TPU v7x, 256 devices: a whole 4x4x8 slice. The times are simulated.
256 devices in a mesh: tok: 32 (over x, z), hid: 8 (over y, core).
Axes of the slice: x: 4, y: 4, z: 8, core: 2. Of those that a mesh axis runs over, the one named last changes fastest.
Arguments:
- tokens: bfloat16 [16384, 5376], P('tok', 'hid'), may hold values from -6 to 6
- norm_gain: bfloat16 [1, 5376], P(None, 'hid'), may hold values from 0.099609375 to 1.8984375
- w_query: bfloat16 [5376, 4096], P('tok', 'hid'), may hold values from -2 to 2
- w_key: bfloat16 [5376, 2048], P('tok', 'hid'), may hold values from -1 to 1
- value_matrix: bfloat16 [5376, 2048], P('tok', 'hid'), may hold values from -0.078125 to 0.078125
- q_norm_gain: bfloat16 [1, 128], replicated, may hold values from 0.1 to 8
- k_norm_gain: bfloat16 [1, 128], replicated, may hold values from 0.1 to 8
- w_out: bfloat16 [4096, 5376], P('hid'), may hold values from -0.125 to 0.125
Outputs:
- attended: bfloat16 [16384, 5376], P('tok', 'hid')
All inputs are finite; a program needn't handle non-finite values.
Results may differ from a plain program's by a relative error of at most 0.017.
Values may be sent and summed in bfloat16 or wider, within the bound.
No kernel may reach another device: no remote copies, remote signals or barrier semaphores. Data moves between devices by JAX's collectives and lax.ppermute only.
A program may use at most 64 MiB of HBM per device.

v0:
```python
import math
import jax
import jax.numpy as jnp
from jax import lax
from jax.sharding import PartitionSpec as P

HEAD_SIZE = 128
WINDOW = 1024
score_scale = 168.0 ** (-0.5)


def shifted(value, axis, steps):
    count = lax.axis_size(axis)
    leading, last = (max(0, -steps), min(count, count - steps))
    return lax.ppermute(value, axis, [(source, source + steps) for source in range(leading, last)])


def head_norm(field, gain):
    count = field.shape[0]
    heads = field.reshape(count, -1, HEAD_SIZE)
    mean_square = jnp.mean(heads * heads, axis=-1, keepdims=True)
    scaled = (
        heads * lax.rsqrt(mean_square + 1e-06) * gain.astype(jnp.float32).reshape(1, 1, HEAD_SIZE)
    )
    return scaled.reshape(count, -1)


def rotate(field, positions):
    count = field.shape[0]
    heads = field.reshape(count, -1, HEAD_SIZE)
    half = HEAD_SIZE // 2
    inverse = jnp.exp(-math.log(10000.0) * jnp.arange(half, dtype=jnp.float32) * 2.0 / HEAD_SIZE)
    angles = positions.astype(jnp.float32)[:, None] * inverse[None, :]
    cosine = jnp.cos(angles)[:, None, :]
    sine = jnp.sin(angles)[:, None, :]
    first = heads[..., :half]
    second = heads[..., half:]
    turned = jnp.concatenate(
        [first * cosine - second * sine, second * cosine + first * sine], axis=-1
    )
    return turned.reshape(count, -1)


def local(tokens, norm_gain, w_query, w_key, value_matrix, q_norm_gain, k_norm_gain, w_out):
    rows = tokens.shape[0]
    gathered, gain_row = (
        lax.all_gather(tokens, "hid", axis=1, tiled=True),
        lax.all_gather(norm_gain, "hid", axis=1, tiled=True),
    )
    values32 = gathered.astype(jnp.float32)
    scale_rows = lax.rsqrt(jnp.mean(values32 * values32, axis=1, keepdims=True) + 1e-06)
    normed = (values32 * scale_rows * gain_row.astype(jnp.float32)).astype(jnp.bfloat16)
    width_query = w_query.shape[1]
    width_kv = w_key.shape[1]
    pieces = (
        lax.all_gather(w_query, "tok", axis=0, tiled=True),
        lax.all_gather(w_key, "tok", axis=0, tiled=True),
        lax.all_gather(value_matrix, "tok", axis=0, tiled=True),
    )
    query_raw, key_raw, value_raw = tuple(
        (jnp.dot(normed, piece, preferred_element_type=jnp.float32) for piece in pieces)
    )
    tok_index = lax.axis_index("tok")
    positions = tok_index * rows + jnp.arange(rows, dtype=jnp.int32)
    query = rotate(head_norm(query_raw, q_norm_gain), positions).astype(jnp.bfloat16)
    key = rotate(head_norm(key_raw, k_norm_gain), positions).astype(jnp.bfloat16)
    value_rows = value_raw.astype(jnp.bfloat16)
    joined = jnp.concatenate([key, value_rows], axis=1)
    reach = (WINDOW - 1 + rows - 1) // rows
    earlier = []
    moving = joined
    for offset in range(reach):
        moving = shifted(moving, "tok", 1)
        earlier = [moving] + earlier
    window_kv = jnp.concatenate(earlier + [joined], axis=0)
    window_extent = window_kv.shape[0]
    key_pos = (tok_index - reach) * rows + jnp.arange(window_extent, dtype=jnp.int32)
    kv_heads = width_kv // HEAD_SIZE
    query_group_count = width_query // HEAD_SIZE // kv_heads
    query_four_axes = query.reshape(rows, kv_heads, query_group_count, HEAD_SIZE)
    keys_three_axes = window_kv[:, :width_kv].reshape(window_extent, kv_heads, HEAD_SIZE)
    values_three_axes = window_kv[:, width_kv:].reshape(window_extent, kv_heads, HEAD_SIZE)
    scores = (
        jnp.einsum(
            "tkgd,skd->kgts", query_four_axes, keys_three_axes, preferred_element_type=jnp.float32
        )
        * score_scale
    )
    allowed = (
        (key_pos[None, :] <= positions[:, None])
        & (key_pos[None, :] > positions[:, None] - WINDOW)
        & (key_pos[None, :] >= 0)
    )
    masked = jnp.where(allowed, scores, -1e30)
    top = jnp.max(masked, axis=-1, keepdims=True)
    weights = jnp.where(allowed, jnp.exp(masked - top), 0.0)
    total = jnp.sum(weights, axis=-1)
    probs = weights.astype(jnp.bfloat16)
    mixed = jnp.einsum(
        "kgts,skd->tkgd", probs, values_three_axes, preferred_element_type=jnp.float32
    )
    mixed = mixed / jnp.transpose(total, (2, 0, 1))[..., None]
    heads_out = mixed.reshape(rows, width_query).astype(jnp.bfloat16)
    partial_value = jnp.dot(heads_out, w_out, preferred_element_type=jnp.float32)
    return lax.psum_scatter(
        partial_value.astype(jnp.bfloat16), "hid", scatter_dimension=1, tiled=True
    )


def solution(mesh):
    in_specs = (
        P("tok", "hid"),
        P(None, "hid"),
        P("tok", "hid"),
        P("tok", "hid"),
        P("tok", "hid"),
        P(),
        P(),
        P("hid", None),
    )
    out_specs = P("tok", "hid")
    return jax.shard_map(local, mesh=mesh, in_specs=in_specs, out_specs=out_specs, check_vma=False)
```

profile of v0, /device:TPU:2, one launch (start us, length us, event | category | flops | bytes accessed | tf_op | source)
XLA Modules:
  0.0 373.7 jit_solution(16431467091909844304)
XLA Ops:
  6.5 0.0 all-gather.5.cloned.1.call-start
  6.5 0.7 all-gather.5.cloned.1.call-update
  7.3 0.0 all-gather.7.cloned.1.call-start
  7.3 0.7 all-gather.7.cloned.1.call-update
  8.0 0.0 all-gather.9.cloned.1.call-start
  8.1 0.7 all-gather.9.cloned.1.call-update
  8.7 0.0 all-gather.11.cloned.1.call-start
  8.8 0.5 all-gather.11.cloned.1.call-update
  9.3 0.0 reduce-scatter.2.cloned.1.call-start
  9.4 1.3 dynamic-slice
  11.3 0.7 reduce
  12.0 0.2 dynamic-update-slice
  12.3 27.5 %all-reduce = bf16[5376]{0:T(1024)(128)(2,1)S(1)} all-reduce(bf16[5376]{0:T(1024)(128)(2,1)S(1)} %dynamic-update-slice), channel_id=1, replica_groups=mesh['tok'=32,'hid'=8] {'hid'}, use_global_device_ids=true, to_apply=%add | all-reduce | flops 5376 | bytes 21504
  39.8 0.7 bitcast_convert_fusion.1
  40.5 0.7 bitcast_convert_fusion
  41.1 0.5 multiply_cosine_fusion
  41.7 10.7 %all-gather.5.cloned.1.call-done = bf16[512,5376]{0,1:T(8,128)(2,1)} async-done(((bf16[512,672]{0,1:T(8,128)(2,1)}), bf16[512,5376]{0,1:T(8,128)(2,1)}) %all-gather.5.cloned.1.call-update) | async-done | bytes 5505040 | tf_op jit(solution)/shard_map/all_gather | solution.py:47
  52.4 3.8 %fusion.1 = f32[512]{0:T(512)S(1)} fusion(bf16[512,5376]{0,1:T(8,128)(2,1)} %all-gather.5.cloned.1.call-done), kind=kLoop, calls=%fused_computation.5 | loop fusion | flops 8257024 | bytes 5507072 | tf_op jit(solution)/shard_map/reduce_sum | solution.py:51
  56.2 76.4 %all-gather.7.cloned.1.call-done = bf16[5376,256]{1,0:T(8,128)(2,1)} async-done(((bf16[168,256]{1,0:T(8,128)(2,1)}), bf16[5376,256]{1,0:T(8,128)(2,1)}) %all-gather.7.cloned.1.call-update) | async-done | bytes 2752528 | tf_op jit(solution)/shard_map/all_gather | solution.py:57
  132.6 5.4 %multiply_reduce_fusion.1 = (f32[512,2]{0,1:T(2,128)S(1)}, f32[512,256]{0,1:T(8,128)S(1)}) fusion(bf16[5376,256]{1,0:T(8,128)(2,1)} %all-gather.7.cloned.1.call-done, bf16[512,5376]{0,1:T(8,128)(2,1)} %all-gather.5.cloned.1.call-done, f32[5376]{0:T(1024)S(1)} %mul.219, f32[512]{0:T(512)S(1)} %add_rsqrt_fusion.2), kind=kOutput, calls=%fused_computation.29 | convolution fusion | flops 1420557312 | bytes 8809472 | tf_op jit(solution)/shard_map/dot_general | solution.py:61
  138.1 0.1 multiply_multiply_fusion.1
  138.2 0.1 subtract_convert_fusion.1
  138.3 72.7 %all-gather.9.cloned.1.call-done = bf16[5376,256]{1,0:T(8,128)(2,1)} async-done(((bf16[168,256]{1,0:T(8,128)(2,1)}), bf16[5376,256]{1,0:T(8,128)(2,1)}) %all-gather.9.cloned.1.call-update) | async-done | bytes 2752528 | tf_op jit(solution)/shard_map/all_gather | solution.py:58
  211.0 5.4 %convolution_convert_fusion.1 = bf16[512,256]{0,1:T(8,128)(2,1)S(1)} fusion(bf16[5376,256]{1,0:T(8,128)(2,1)} %all-gather.9.cloned.1.call-done, bf16[512,5376]{0,1:T(8,128)(2,1)} %all-gather.5.cloned.1.call-done, f32[5376]{0:T(1024)S(1)} %mul.219, f32[512]{0:T(512)S(1)} %add_rsqrt_fusion.2), kind=kOutput, calls=%fused_computation.21 | convolution fusion | flops 1420427264 | bytes 8543232 | tf_op jit(solution)/shard_map/dot_general | solution.py:61
  216.5 2.9 collective-permute-start
  219.4 1.1 and_and_fusion
  220.6 10.4 %collective-permute-done = bf16[512,512]{0,1:T(8,128)(2,1)S(1)} collective-permute-done((bf16[512,512]{0,1:T(8,128)(2,1)S(1)}, bf16[512,512]{0,1:T(8,128)(2,1)S(1)}, u32[]{:S(2)}, u32[]{:S(2)}) %collective-permute-start) | collective-permute-done | bytes 524320 | tf_op jit(solution)/shard_map/ppermute | solution.py:15
  231.0 2.1 collective-permute-start.1
  233.1 63.4 %all-gather.11.cloned.1.call-done = bf16[5376,512]{1,0:T(8,128)(2,1)} async-done(((bf16[168,512]{1,0:T(8,128)(2,1)}), bf16[5376,512]{1,0:T(8,128)(2,1)}) %all-gather.11.cloned.1.call-update) | async-done | bytes 5505040 | tf_op jit(solution)/shard_map/all_gather | solution.py:56
  296.5 7.6 %multiply_reduce_fusion = (f32[512,4]{0,1:T(4,128)S(1)}, f32[512,512]{0,1:T(8,128)S(1)}) fusion(bf16[5376,512]{1,0:T(8,128)(2,1)} %all-gather.11.cloned.1.call-done, bf16[512,5376]{0,1:T(8,128)(2,1)} %all-gather.5.cloned.1.call-done, f32[5376]{0:T(1024)S(1)} %mul.219, f32[512]{0:T(512)S(1)} %add_rsqrt_fusion.2), kind=kOutput, calls=%fused_computation.23 | convolution fusion | flops 2830104576 | bytes 12090368 | tf_op jit(solution)/shard_map/dot_general | solution.py:61
  304.1 0.2 multiply_multiply_fusion
  304.3 0.2 subtract_convert_fusion
  304.6 0.0 collective-permute-done.1
  304.6 0.1 maximum_maximum_fusion
  304.7 0.1 fusion.30
  304.8 8.5 %fusion.31 = (f32[2,2,512]{2,1,0:T(2,128)S(1)}, bf16[2,2,512,1536]{2,3,1,0:T(8,128)(2,1)}) fusion(pred[512,1536]{0,1:T(8,128)(4,1)S(1)} %and_and_fusion, bf16[1536,2,128,1]{0,2,3,1:T(8,128)(2,1)S(1)} %bitcast.59, bf16[512,2,2,128]{0,3,2,1:T(8,128)(2,1)S(1)} %bitcast.60), kind=kOutput, calls=%fused_computation.51 | convolution fusion | flops 824182272 | bytes 8396800 | tf_op jit(solution)/shard_map/sub | solution.py:96
  313.3 3.8 %fusion.18 = bf16[512,2,2,128]{0,3,2,1:T(8,128)(2,1)S(1)} fusion(bf16[1536,2,128,1]{0,2,3,1:T(8,128)(2,1)S(1)} %bitcast.58, bf16[2,2,512,1536]{2,3,1,0:T(8,128)(2,1)} %get-tuple-element.18, f32[512,2,2]{0,2,1:T(2,128)S(1)} %bitcast.62), kind=kOutput, calls=%fused_computation.20 | convolution fusion | flops 805830656 | bytes 7610368 | tf_op jit(solution)/shard_map/kgts,skd->tkgd/dot_general | solution.py:99
  317.1 8.6 %convolution_convert_fusion = bf16[512,5376]{0,1:T(8,128)(2,1)} fusion(bf16[512,512]{0,1:T(8,128)(2,1)S(1)} %bitcast.61, bf16[512,5376]{1,0:T(8,128)(2,1)} %param.15), kind=kOutput, calls=%fused_computation.9 | convolution fusion | flops 2821324800 | bytes 11534336 | tf_op jit(solution)/shard_map/dot_general | solution.py:104
  325.7 0.0 reduce-scatter.2.cloned.1.call-update
  325.7 41.5 %reduce-scatter.2.cloned.1.call-done = bf16[512,672]{0,1:T(8,128)(2,1)} async-done(((bf16[512,5376]{0,1:T(8,128)(2,1)}), bf16[512,672]{0,1:T(8,128)(2,1)}) %reduce-scatter.2.cloned.1.call-update) | async-done | bytes 688144 | tf_op jit(solution)/shard_map/reduce_scatter | solution.py:105
  (13 shorter events, 0.2 us)
Async XLA Ops:
  6.5 45.9 %all-gather.5.cloned.1.call-start = ((), (), s32[]{:S(2)}) async-start(), calls=%async_computation.1 | async-start | bytes 6193152 | tf_op jit(solution)/shard_map/all_gather | solution.py:47
  7.3 125.3 %all-gather.7.cloned.1.call-start = ((), (), s32[]{:S(2)}) async-start(), calls=%async_computation.2 | async-start | bytes 2838528 | tf_op jit(solution)/shard_map/all_gather | solution.py:57
  8.0 203.0 %all-gather.9.cloned.1.call-start = ((), (), s32[]{:S(2)}) async-start(), calls=%async_computation.3 | async-start | bytes 2838528 | tf_op jit(solution)/shard_map/all_gather | solution.py:58
  8.7 287.8 %all-gather.11.cloned.1.call-start = ((), (), s32[]{:S(2)}) async-start(), calls=%async_computation.4 | async-start | bytes 5677056 | tf_op jit(solution)/shard_map/all_gather | solution.py:56
  9.3 357.9 %reduce-scatter.2.cloned.1.call-start = ((), (), s32[]{:S(2)}) async-start(), calls=%async_computation.5 | async-start | bytes 6193152 | tf_op jit(solution)/shard_map/reduce_scatter | solution.py:105
  216.5 14.5 %collective-permute-start = (bf16[512,512]{0,1:T(8,128)(2,1)S(1)}, bf16[512,512]{0,1:T(8,128)(2,1)S(1)}, u32[]{:S(2)}, u32[]{:S(2)}) collective-permute-start(bf16[512,512]{0,1:T(8,128)(2,1)S(1)} %pad_maximum_fusion), channel_id=1, source_target_pairs={{0,8},{8,16},{16,24},{24,32},{32,40},{40,48},{48,56},{56,64},{64,7... | collective-permute-start | bytes 1572872 | tf_op jit(solution)/shard_map/ppermute | solution.py:15
  231.0 73.5 %collective-permute-start.1 = (bf16[512,512]{0,1:T(8,128)(2,1)S(1)}, bf16[512,512]{0,1:T(8,128)(2,1)S(1)}, u32[]{:S(2)}, u32[]{:S(2)}) collective-permute-start(bf16[512,512]{0,1:T(8,128)(2,1)S(1)} %collective-permute-done), channel_id=1, source_target_pairs={{0,8},{8,16},{16,24},{24,32},{32,40},{40,48},{48,56},{56,64},{64,7... | collective-permute-start | bytes 1572872 | tf_op jit(solution)/shard_map/ppermute | solution.py:15
Sparse Core Ops, SparseCore 0:
  9.2 43.1 all-gather.4
  55.0 77.5 all-gather.6
  135.2 75.7 all-gather.8
  213.4 83.0 all-gather.10
  325.9 41.3 reduce-scatter.1
where the time goes:
time: 374 us
  waiting for transfers between devices  278 us (74%)
  matrix products  39.4 us (11%)
  blocking collectives  27.5 us (7%)
  between operations  14 us (4%)
  other arithmetic  8.29 us (2%)
  starting transfers between devices  5.17 us (1%)
    all_gather x1, waiting for transfers between devices, local(): lax.all_gather(w_key, 'tok', axis=0, tiled=True)  76.4 us
    all_gather x1, waiting for transfers between devices, local(): lax.all_gather(value_matrix, 'tok', axis=0, tiled=True)  72.7 us
    all_gather x1, waiting for transfers between devices, local(): lax.all_gather(w_query, 'tok', axis=0, tiled=True)  63.4 us
    reduce_scatter x1, waiting for transfers between devices, local(): lax.psum_scatter(partial_value.astype(jnp.bfloat16), 'hid', scatter_dimen...  41.5 us
    unnamed x1, blocking collectives  27.5 us
    dot_general x3, matrix products, local(): jnp.dot(normed, piece, preferred_element_type=jnp.float32)  18.5 us
    all_gather x1, waiting for transfers between devices, local(): lax.all_gather(tokens, 'hid', axis=1, tiled=True)  10.7 us
    ppermute x2, waiting for transfers between devices, shifted(): lax.ppermute(value, axis, [(source, source + steps) for source in range(l...  10.4 us
  transfers between devices with their start and end apart: 7, of which 6 were waited for; matrix products, arithmetic and copies ran while one was open for 8% of the time, Pallas kernels for 0%

commit v1 on v0

--- a/solution.py
+++ b/solution.py
@@ -54,7 +54,9 @@
     width_kv = w_key.shape[1]
     pieces = (
         lax.all_gather(w_query, "tok", axis=0, tiled=True),
-        lax.all_gather(w_key, "tok", axis=0, tiled=True),
+        jnp.concatenate(
+            lax.all_to_all(jnp.stack([w_key] * lax.axis_size("tok")), "tok", 0, 0), axis=0
+        ),
         lax.all_gather(value_matrix, "tok", axis=0, tiled=True),
     )
     query_raw, key_raw, value_raw = tuple(

time: 374 us -> 299 us (0.80)
  waiting for transfers between devices: 278 us -> 188 us
  starting transfers between devices: 5.17 us -> 16.8 us
  local copies, waits for them, and re-layouts: 1.62 us -> 6.79 us
    all_gather x1 -> x0, waiting for transfers between devices: 76.4 us -> none  [local(): lax.all_gather(w_key, 'tok', axis=0, tiled=True)]
    all_gather x1, waiting for transfers between devices: 72.7 us -> 37 us  [local(): lax.all_gather(value_matrix, 'tok', axis=0, tiled=True)]
    all_to_all x0 -> x1, waiting for transfers between devices: none -> 33.7 us  [local(): lax.all_to_all(jnp.stack([w_key] * lax.axis_size('tok')), 'tok', 0, 0)]
    all_to_all x0 -> x1, starting transfers between devices: none -> 11.6 us  [local(): lax.all_to_all(jnp.stack([w_key] * lax.axis_size('tok')), 'tok', 0, 0)]
    all_gather x1, waiting for transfers between devices: 10.7 us -> 0.01 us  [local(): lax.all_gather(tokens, 'hid', axis=1, tiled=True)]
  transfers between devices with their start and end apart: 7 -> 7, of which waited for: 6 -> 5; matrix products, arithmetic and copies ran while one was open for 8% -> 10% of each run, Pallas kernels for 0% -> 0%
where the time goes in v1:
time: 299 us
  waiting for transfers between devices  188 us (63%)
  matrix products  37.6 us (13%)
  blocking collectives  28.3 us (9%)
  starting transfers between devices  16.8 us (6%)
  between operations  14 us (5%)
  other arithmetic  7.49 us (3%)
  local copies, waits for them, and re-layouts  6.79 us (2%)
    all_gather x1, waiting for transfers between devices, local(): lax.all_gather(w_query, 'tok', axis=0, tiled=True)  63.4 us
    reduce_scatter x1, waiting for transfers between devices, local(): lax.psum_scatter(partial_value.astype(jnp.bfloat16), 'hid', scatter_dimen...  41.4 us
    all_gather x1, waiting for transfers between devices, local(): lax.all_gather(value_matrix, 'tok', axis=0, tiled=True)  37 us
    all_to_all x1, waiting for transfers between devices, local(): lax.all_to_all(jnp.stack([w_key] * lax.axis_size('tok')), 'tok', 0, 0)  33.7 us
    unnamed x1, blocking collectives  28.3 us
    dot_general x3, matrix products, local(): jnp.dot(normed, piece, preferred_element_type=jnp.float32)  16.7 us
    all_to_all x1, starting transfers between devices, local(): lax.all_to_all(jnp.stack([w_key] * lax.axis_size('tok')), 'tok', 0, 0)  11.6 us
    ppermute x2, waiting for transfers between devices, shifted(): lax.ppermute(value, axis, [(source, source + steps) for source in range(l...  10.4 us
  transfers between devices with their start and end apart: 7, of which 5 were waited for; matrix products, arithmetic and copies ran while one was open for 10% of the time, Pallas kernels for 0%

profile of v1, /device:TPU:2, one launch (start us, length us, event | category | flops | bytes accessed | tf_op | source)
XLA Modules:
  0.0 299.0 jit_solution(5108339447238413619)
XLA Ops:
  6.5 0.0 copy-start.4
  6.5 0.0 copy-start.1
  6.5 0.0 copy-start.2
  6.5 0.0 copy-start.3
  6.5 0.0 all-gather.4.cloned.1.call-start
  6.6 0.7 all-gather.4.cloned.1.call-update
  7.3 0.0 all-gather.6.cloned.1.call-start
  7.3 0.7 all-gather.6.cloned.1.call-update
  8.0 0.0 all-gather.8.cloned.1.call-start
  8.1 0.7 all-gather.8.cloned.1.call-update
  8.8 2.6 stack.2
  11.3 11.6 %all-to-all-start = ((bf16[32,168,256]{2,1,0:T(8,128)(2,1)}), bf16[32,168,256]{2,1,0:T(8,128)(2,1)S(1)}, u32[]{:S(2)}, u32[]{:S(2)}) async-start(bf16[32,168,256]{2,1,0:T(8,128)(2,1)} %stack.2), calls=%async_computation | async-start | bytes 5505024 | tf_op jit(solution)/shard_map/all_to_all | solution.py:58
  23.0 0.0 reduce-scatter.2.cloned.1.call-start
  23.0 0.0 copy-done.4
  23.0 0.6 dynamic-slice
  24.3 0.0 copy-done.1
  24.3 0.2 dynamic-update-slice
  24.6 28.3 %all-reduce = bf16[5376]{0:T(1024)(128)(2,1)S(1)} all-reduce(bf16[5376]{0:T(1024)(128)(2,1)S(1)} %dynamic-update-slice), channel_id=1, replica_groups=mesh['tok'=32,'hid'=8] {'hid'}, use_global_device_ids=true, to_apply=%add | all-reduce | flops 5376 | bytes 21504
  52.9 0.0 copy-done.2
  52.9 0.0 copy-done.3
  52.9 0.5 multiply_cosine_fusion
  53.5 33.7 %all-to-all-done = bf16[32,168,256]{2,1,0:T(8,128)(2,1)S(1)} async-done(((bf16[32,168,256]{2,1,0:T(8,128)(2,1)}), bf16[32,168,256]{2,1,0:T(8,128)(2,1)S(1)}, u32[]{:S(2)}, u32[]{:S(2)}) %all-to-all-start) | async-done | bytes 2752544 | tf_op jit(solution)/shard_map/all_to_all | solution.py:58
  87.2 3.0 %copy.14 = bf16[256,5376]{1,0:T(8,128)(2,1)} copy(bf16[256,5376]{0,1:T(8,128)(2,1)S(1)} %bitcast.62) | data formatting | bytes 5505024 | tf_op jit(solution)/shard_map/dot_general | solution.py:63
  90.2 0.0 all-gather.4.cloned.1.call-done
  90.2 0.0 copy-start
  90.2 3.9 %fusion.1 = f32[512]{0:T(512)S(1)} fusion(bf16[512,5376]{0,1:T(8,128)(2,1)} %all-gather.4.cloned.1.call-done), kind=kLoop, calls=%fused_computation.5 | loop fusion | flops 8257024 | bytes 5507072 | tf_op jit(solution)/shard_map/reduce_sum | solution.py:51
  94.1 0.3 copy-done
  94.4 3.7 %multiply_reduce_fusion.1 = (f32[512,2]{0,1:T(2,128)S(1)}, f32[512,2,128]{0,2,1:T(8,128)S(1)}) fusion(bf16[2,128,5376]{2,1,0:T(8,128)(2,1)} %bitcast.63, f32[5376]{0:T(1024)S(1)} %mul.219, f32[512]{0:T(512)S(1)} %add_rsqrt_fusion.2, bf16[512,5376]{0,1:T(8,128)(2,1)S(1)} %copy-done), kind=kOutput, calls=%fused_computation.31 | convolution fusion | flops 1420557312 | bytes 8809472 | tf_op jit(solution)/shard_map/dot_general | solution.py:63
  98.1 0.1 multiply_multiply_fusion.1
  98.2 0.1 subtract_convert_fusion.1
  98.3 37.0 %all-gather.6.cloned.1.call-done = bf16[5376,256]{1,0:T(8,128)(2,1)} async-done(((bf16[168,256]{1,0:T(8,128)(2,1)}), bf16[5376,256]{1,0:T(8,128)(2,1)}) %all-gather.6.cloned.1.call-update) | async-done | bytes 2752528 | tf_op jit(solution)/shard_map/all_gather | solution.py:60
  135.3 5.4 %convolution_convert_fusion.1 = bf16[512,256]{0,1:T(8,128)(2,1)S(1)} fusion(bf16[5376,256]{1,0:T(8,128)(2,1)} %all-gather.6.cloned.1.call-done, bf16[512,5376]{0,1:T(8,128)(2,1)} %all-gather.4.cloned.1.call-done, f32[5376]{0:T(1024)S(1)} %mul.219, f32[512]{0:T(512)S(1)} %add_rsqrt_fusion.2), kind=kOutput, calls=%fused_computation.23 | convolution fusion | flops 1420427264 | bytes 8543232 | tf_op jit(solution)/shard_map/dot_general | solution.py:63
  140.8 2.9 collective-permute-start
  143.7 1.1 and_and_fusion
  144.9 10.4 %collective-permute-done = bf16[512,512]{0,1:T(8,128)(2,1)S(1)} collective-permute-done((bf16[512,512]{0,1:T(8,128)(2,1)S(1)}, bf16[512,512]{0,1:T(8,128)(2,1)S(1)}, u32[]{:S(2)}, u32[]{:S(2)}) %collective-permute-start) | collective-permute-done | bytes 524320 | tf_op jit(solution)/shard_map/ppermute | solution.py:15
  155.3 2.1 collective-permute-start.1
  157.4 63.4 %all-gather.8.cloned.1.call-done = bf16[5376,512]{1,0:T(8,128)(2,1)} async-done(((bf16[168,512]{1,0:T(8,128)(2,1)}), bf16[5376,512]{1,0:T(8,128)(2,1)}) %all-gather.8.cloned.1.call-update) | async-done | bytes 5505040 | tf_op jit(solution)/shard_map/all_gather | solution.py:56
  220.8 7.6 %multiply_reduce_fusion = (f32[512,4]{0,1:T(4,128)S(1)}, f32[512,512]{0,1:T(8,128)S(1)}) fusion(bf16[5376,512]{1,0:T(8,128)(2,1)} %all-gather.8.cloned.1.call-done, bf16[512,5376]{0,1:T(8,128)(2,1)} %all-gather.4.cloned.1.call-done, f32[5376]{0:T(1024)S(1)} %mul.219, f32[512]{0:T(512)S(1)} %add_rsqrt_fusion.2), kind=kOutput, calls=%fused_computation.25 | convolution fusion | flops 2830104576 | bytes 12090368 | tf_op jit(solution)/shard_map/dot_general | solution.py:63
  228.5 0.2 multiply_multiply_fusion
  228.7 0.2 subtract_convert_fusion
  228.9 0.0 collective-permute-done.1
  228.9 1.1 maximum_maximum_fusion
  230.0 0.1 fusion.31
  230.1 8.5 %fusion.32 = (f32[2,2,512]{2,1,0:T(2,128)S(1)}, bf16[2,2,512,1536]{2,3,1,0:T(8,128)(2,1)}) fusion(pred[512,1536]{0,1:T(8,128)(4,1)S(1)} %and_and_fusion, bf16[1536,2,128,1]{0,2,3,1:T(8,128)(2,1)S(1)} %bitcast.67, bf16[512,2,2,128]{0,3,2,1:T(8,128)(2,1)S(1)} %bitcast.68), kind=kOutput, calls=%fused_computation.52 | convolution fusion | flops 824182272 | bytes 8396800 | tf_op jit(solution)/shard_map/sub | solution.py:98
  238.7 3.8 %fusion.20 = bf16[512,2,2,128]{0,3,2,1:T(8,128)(2,1)S(1)} fusion(bf16[1536,2,128,1]{0,2,3,1:T(8,128)(2,1)S(1)} %bitcast.66, bf16[2,2,512,1536]{2,3,1,0:T(8,128)(2,1)} %get-tuple-element.18, f32[512,2,2]{0,2,1:T(2,128)S(1)} %bitcast.70), kind=kOutput, calls=%fused_computation.22 | convolution fusion | flops 805830656 | bytes 7610368 | tf_op jit(solution)/shard_map/kgts,skd->tkgd/dot_general | solution.py:101
  242.4 8.6 %convolution_convert_fusion = bf16[512,5376]{0,1:T(8,128)(2,1)} fusion(bf16[512,512]{0,1:T(8,128)(2,1)S(1)} %bitcast.69, bf16[512,5376]{1,0:T(8,128)(2,1)} %param.15), kind=kOutput, calls=%fused_computation.9 | convolution fusion | flops 2821324800 | bytes 11534336 | tf_op jit(solution)/shard_map/dot_general | solution.py:106
  251.1 0.0 reduce-scatter.2.cloned.1.call-update
  251.1 41.4 %reduce-scatter.2.cloned.1.call-done = bf16[512,672]{0,1:T(8,128)(2,1)} async-done(((bf16[512,5376]{0,1:T(8,128)(2,1)}), bf16[512,672]{0,1:T(8,128)(2,1)}) %reduce-scatter.2.cloned.1.call-update) | async-done | bytes 688144 | tf_op jit(solution)/shard_map/reduce_scatter | solution.py:107
  (16 shorter events, 0.2 us)
Async XLA Ops:
  6.5 16.5 %copy-start.4 = (u32[256]{0:T(256)S(1)}, u32[256]{0:T(256)}, u32[]{:S(2)}) copy-start(u32[256]{0:T(256)} %constant.48) | copy-start | bytes 3076
  6.5 17.7 %copy-start.1 = (bf16[1,672]{1,0:T(2,128)(2,1)S(1)}, bf16[1,672]{1,0:T(2,128)(2,1)}, u32[]{:S(2)}) copy-start(bf16[1,672]{1,0:T(2,128)(2,1)} %param.9) | copy-start | bytes 4036
  6.5 46.3 %copy-start.2 = (bf16[1,128]{1,0:T(2,128)(2,1)S(1)}, bf16[1,128]{1,0:T(2,128)(2,1)}, u32[]{:S(2)}) copy-start(bf16[1,128]{1,0:T(2,128)(2,1)} %param.14) | copy-start | bytes 772
  6.5 46.4 %copy-start.3 = (bf16[1,128]{1,0:T(2,128)(2,1)S(1)}, bf16[1,128]{1,0:T(2,128)(2,1)}, u32[]{:S(2)}) copy-start(bf16[1,128]{1,0:T(2,128)(2,1)} %param.13) | copy-start | bytes 772
  6.5 83.6 %all-gather.4.cloned.1.call-start = ((), (), s32[]{:S(2)}) async-start(), calls=%async_computation.2 | async-start | bytes 6193152 | tf_op jit(solution)/shard_map/all_gather | solution.py:47
  7.3 128.0 %all-gather.6.cloned.1.call-start = ((), (), s32[]{:S(2)}) async-start(), calls=%async_computation.3 | async-start | bytes 2838528 | tf_op jit(solution)/shard_map/all_gather | solution.py:60
  8.0 212.8 %all-gather.8.cloned.1.call-start = ((), (), s32[]{:S(2)}) async-start(), calls=%async_computation.4 | async-start | bytes 5677056 | tf_op jit(solution)/shard_map/all_gather | solution.py:56
  11.3 75.8 %all-to-all-start = ((bf16[32,168,256]{2,1,0:T(8,128)(2,1)}), bf16[32,168,256]{2,1,0:T(8,128)(2,1)S(1)}, u32[]{:S(2)}, u32[]{:S(2)}) async-start(bf16[32,168,256]{2,1,0:T(8,128)(2,1)} %stack.2), calls=%async_computation | async-start | bytes 5505024 | tf_op jit(solution)/shard_map/all_to_all | solution.py:58
  23.0 269.5 %reduce-scatter.2.cloned.1.call-start = ((), (), s32[]{:S(2)}) async-start(), calls=%async_computation.5 | async-start | bytes 6193152 | tf_op jit(solution)/shard_map/reduce_scatter | solution.py:107
  90.2 4.2 %copy-start = (bf16[512,5376]{0,1:T(8,128)(2,1)S(1)}, bf16[512,5376]{0,1:T(8,128)(2,1)}, u32[]{:S(2)}) copy-start(bf16[512,5376]{0,1:T(8,128)(2,1)} %all-gather.4.cloned.1.call-done) | copy-start | bytes 16515076
  140.8 14.5 %collective-permute-start = (bf16[512,512]{0,1:T(8,128)(2,1)S(1)}, bf16[512,512]{0,1:T(8,128)(2,1)S(1)}, u32[]{:S(2)}, u32[]{:S(2)}) collective-permute-start(bf16[512,512]{0,1:T(8,128)(2,1)S(1)} %pad_maximum_fusion), channel_id=1, source_target_pairs={{0,8},{8,16},{16,24},{24,32},{32,40},{40,48},{48,56},{56,64},{64,7... | collective-permute-start | bytes 1572872 | tf_op jit(solution)/shard_map/ppermute | solution.py:15
  155.3 73.6 %collective-permute-start.1 = (bf16[512,512]{0,1:T(8,128)(2,1)S(1)}, bf16[512,512]{0,1:T(8,128)(2,1)}, u32[]{:S(2)}, u32[]{:S(2)}) collective-permute-start(bf16[512,512]{0,1:T(8,128)(2,1)S(1)} %collective-permute-done), channel_id=1, source_target_pairs={{0,8},{8,16},{16,24},{24,32},{32,40},{40,48},{48,56},{56,64},{64,7... | collective-permute-start | bytes 1572872 | tf_op jit(solution)/shard_map/ppermute | solution.py:15
Sparse Core Ops, SparseCore 0:
  9.2 43.3 all-gather.3
  55.2 80.0 all-gather.5
  137.9 82.9 all-gather.7
  251.2 41.2 reduce-scatter.1
